TPU v7x, 32 devices: a whole 2x2x4 slice. The times are simulated.
32 devices in a mesh: dp: 4 (over z), ctx: 8 (over y, x, core).
Axes of the slice: x: 2, y: 2, z: 4, core: 2. Of those that a mesh axis runs over, the one named last changes fastest.
Arguments:
- tokens: bfloat16 [4, 1024, 6144], P('dp', 'ctx'), may hold values from -0.1875 to 0.1875
- cotangent: bfloat16 [4, 1024, 6144], P('dp', 'ctx'), may hold values from -6 to 6
- w_router: float32 [6144], replicated, may hold values from -2 to 2
- w_query: bfloat16 [6144, 4096], P(None, 'ctx'), may hold values from -0.078125 to 0.078125
- w_key: bfloat16 [6144, 4096], P(None, 'ctx'), may hold values from -0.078125 to 0.078125
- w_value: bfloat16 [6144, 4096], P(None, 'ctx'), may hold values from -0.078125 to 0.078125
- w_out: bfloat16 [4096, 6144], P('ctx'), may hold values from -0.09375 to 0.09375
- chosen: int32 [4, 160], P('dp', 'ctx'), may hold values from -1 to 1023, as said below
- counts: int32 [4, 8], P('dp', 'ctx'), may hold values from 12 to 20, as said below
Outputs:
- layer_out: bfloat16 [4, 1024, 6144], P('dp', 'ctx')
- grad_query: bfloat16 [6144, 4096], P('dp', 'ctx')
- grad_key: bfloat16 [6144, 4096], P('dp', 'ctx')
- grad_value: bfloat16 [6144, 4096], P('dp', 'ctx')
- grad_out: bfloat16 [4096, 6144], P('ctx', 'dp')
- grad_router: float32 [6144], replicated
Inputs may be any that keep to these rules, and one draw needn't show every extreme that they name: `chosen`: for every sequence b and device block c, the first counts[b, c] of the block's slots c * 20 to (c + 1) * 20 - 1 hold increasing positions of that device's tokens, c * 128 to (c + 1) * 128 - 1; the other slots hold -1. In every sequence the counts add up to 128, and some device's block has exactly 20 used slots.
All inputs are finite; a program needn't handle non-finite values.
Results may differ from a plain program's by a relative error of at most 0.018.
Values may be sent and summed in bfloat16 or wider, within the bound.
No kernel may reach another device: no remote copies, remote signals or barrier semaphores. Data moves between devices by JAX's collectives and lax.ppermute only.
A program may use at most 128 MiB of HBM per device.

v0:
```python
import math
import jax
import jax.numpy as jnp
from jax import lax
from jax.sharding import PartitionSpec as P

HDIM = 128
HIGHEST_PRECISION = lax.Precision.HIGHEST
ROW_CONTRACT = (((0,), (0,)), ((), ()))
COLUMN_CONTRACT = (((1,), (1,)), ((), ()))


def head_norm(values, width):
    shaped = values.reshape(values.shape[0], -1, width)
    inverse = lax.rsqrt(jnp.mean(shaped * shaped, axis=-1, keepdims=True) + 1e-06)
    return (shaped * inverse, inverse)


def norm_back(grad_hat, normal, inverse):
    return inverse * (grad_hat - normal * jnp.mean(grad_hat * normal, axis=-1, keepdims=True))


def rounded_term(part):
    return lax.optimization_barrier(part.astype(jnp.bfloat16)).astype(jnp.float32)


def body(tokens, cotangent, w_router, w_query, w_key, w_value, w_out, chosen, counts):
    length = tokens.shape[1]
    capacity = chosen.shape[1]
    inner = w_query.shape[1]
    heads_here = inner // HDIM
    scale = 1.0 / math.sqrt(HDIM)
    offset = lax.axis_index("ctx") * length
    slot_ids = lax.broadcasted_iota(jnp.int32, (capacity,), 0)
    local = chosen[0] - offset
    present = (slot_ids < counts[0, 0]) & (local >= 0) & (local < length)
    columns = lax.broadcasted_iota(jnp.int32, (capacity, length), 1)
    onehot = ((local[:, None] == columns) & present[:, None]).astype(jnp.bfloat16)
    rows = jnp.dot(onehot, tokens[0], preferred_element_type=jnp.float32)
    rows_back = jnp.dot(onehot, cotangent[0], preferred_element_type=jnp.float32)
    logits = jnp.dot(rows, w_router, precision=HIGHEST_PRECISION)
    weights = jax.nn.sigmoid(logits)
    normed = (rows * lax.rsqrt(jnp.mean(rows * rows, axis=-1, keepdims=True) + 1e-05)).astype(
        jnp.bfloat16
    )
    delta = (weights[:, None] * rows_back).astype(jnp.bfloat16)
    all_normed, all_delta, all_present = (
        lax.all_gather(normed, "ctx", axis=0, tiled=True),
        lax.all_gather(delta, "ctx", axis=0, tiled=True),
        lax.all_gather(present.astype(jnp.bfloat16), "ctx", axis=0, tiled=True),
    )
    slots = all_normed.shape[0]
    query_raw = jnp.dot(all_normed, w_query, preferred_element_type=jnp.float32)
    key_raw = jnp.dot(all_normed, w_key, preferred_element_type=jnp.float32)
    value_raw = jnp.dot(all_normed, w_value, preferred_element_type=jnp.float32)
    query_hat, query_scale = head_norm(query_raw, HDIM)
    key_hat, key_scale = head_norm(key_raw, HDIM)
    query_b = query_hat.astype(jnp.bfloat16)
    key_b = key_hat.astype(jnp.bfloat16)
    value_b = value_raw.reshape(slots, heads_here, HDIM).astype(jnp.bfloat16)
    current = lax.broadcasted_iota(jnp.int32, (slots, slots), 0)
    earlier = lax.broadcasted_iota(jnp.int32, (slots, slots), 1)
    allowed = (earlier <= current) & ((all_present[None, :] > 0.5) | (earlier == current))
    scores = jnp.einsum("ihd,jhd->hij", query_b, key_b, preferred_element_type=jnp.float32) * scale
    exponent = jnp.where(allowed[None], jnp.exp(scores), 0.0)
    attend = exponent / jnp.sum(exponent, axis=-1, keepdims=True)
    attend_b = attend.astype(jnp.bfloat16)
    mixed = jnp.einsum("hij,jhd->ihd", attend_b, value_b, preferred_element_type=jnp.float32)
    mixed = mixed.astype(jnp.bfloat16).reshape(slots, inner)
    update = lax.psum_scatter(
        rounded_term(jnp.dot(mixed, w_out, preferred_element_type=jnp.float32)).astype(
            jnp.bfloat16
        ),
        "ctx",
        scatter_dimension=0,
        tiled=True,
    ).astype(jnp.float32)
    scaled = weights[:, None] * update
    spread = jnp.dot(onehot.astype(jnp.float32).T, scaled, precision=HIGHEST_PRECISION)
    layer_out = (tokens[0].astype(jnp.float32) + spread).astype(jnp.bfloat16)[None]
    gate_back = jnp.sum(rows_back * update, axis=-1) * weights * (1.0 - weights)
    router_part = jnp.dot(gate_back, rows, precision=HIGHEST_PRECISION)
    grad_router = lax.psum(router_part, ("dp", "ctx"))
    out_term = rounded_term(
        lax.dot_general(mixed, all_delta, ROW_CONTRACT, preferred_element_type=jnp.float32)
    )
    mixed_back = lax.dot_general(
        all_delta, w_out, COLUMN_CONTRACT, preferred_element_type=jnp.float32
    )
    mixed_back = mixed_back.astype(jnp.bfloat16).reshape(slots, heads_here, HDIM)
    attend_back = jnp.einsum(
        "ihd,jhd->hij", mixed_back, value_b, preferred_element_type=jnp.float32
    )
    inner_sum = jnp.sum(attend * attend_back, axis=-1, keepdims=True)
    scores_back = (attend * (attend_back - inner_sum) * scale).astype(jnp.bfloat16)
    value_back = jnp.einsum(
        "hij,ihd->jhd", attend_b, mixed_back, preferred_element_type=jnp.float32
    )
    value_back = value_back.astype(jnp.bfloat16).reshape(slots, inner)
    qhat_back = jnp.einsum("hij,jhd->ihd", scores_back, key_b, preferred_element_type=jnp.float32)
    khat_back = jnp.einsum("hij,ihd->jhd", scores_back, query_b, preferred_element_type=jnp.float32)
    query_back = (
        norm_back(qhat_back, query_hat, query_scale).astype(jnp.bfloat16).reshape(slots, inner)
    )
    key_back = norm_back(khat_back, key_hat, key_scale).astype(jnp.bfloat16).reshape(slots, inner)
    query_term = rounded_term(
        lax.dot_general(all_normed, query_back, ROW_CONTRACT, preferred_element_type=jnp.float32)
    )
    key_term = rounded_term(
        lax.dot_general(all_normed, key_back, ROW_CONTRACT, preferred_element_type=jnp.float32)
    )
    value_term = rounded_term(
        lax.dot_general(all_normed, value_back, ROW_CONTRACT, preferred_element_type=jnp.float32)
    )
    grad_query, grad_key, grad_value, grad_out = (
        lax.psum_scatter(
            query_term.astype(jnp.bfloat16), "dp", scatter_dimension=0, tiled=True
        ).astype(jnp.float32),
        lax.psum_scatter(
            key_term.astype(jnp.bfloat16), "dp", scatter_dimension=0, tiled=True
        ).astype(jnp.float32),
        lax.psum_scatter(
            value_term.astype(jnp.bfloat16), "dp", scatter_dimension=0, tiled=True
        ).astype(jnp.float32),
        lax.psum_scatter(
            out_term.astype(jnp.bfloat16), "dp", scatter_dimension=1, tiled=True
        ).astype(jnp.float32),
    )
    return (
        layer_out,
        grad_query.astype(jnp.bfloat16),
        grad_key.astype(jnp.bfloat16),
        grad_value.astype(jnp.bfloat16),
        grad_out.astype(jnp.bfloat16),
        grad_router,
    )


def solution(mesh):
    in_specs = (
        P("dp", "ctx", None),
        P("dp", "ctx", None),
        P(),
        P(None, "ctx"),
        P(None, "ctx"),
        P(None, "ctx"),
        P("ctx", None),
        P("dp", "ctx"),
        P("dp", "ctx"),
    )
    out_specs = (
        P("dp", "ctx", None),
        P("dp", "ctx"),
        P("dp", "ctx"),
        P("dp", "ctx"),
        P("ctx", "dp"),
        P(),
    )
    return jax.shard_map(body, mesh=mesh, in_specs=in_specs, out_specs=out_specs, check_vma=False)
```

profile of v0, /device:TPU:0, one launch (start us, length us, event | category | flops | bytes accessed | tf_op | source)
XLA Modules:
  0.0 630.2 jit_solution(3186163892697100419)
XLA Ops:
  7.2 0.0 copy-start
  7.2 0.0 all-gather.5.cloned.1.call-start
  8.0 0.7 fusion.88
  8.7 1.9 multiply_reduce_fusion.1
  10.6 0.9 fusion.31
  11.5 0.0 all-gather.5.cloned.1.call-update
  11.5 0.0 all-gather.7.cloned.1.call-start
  11.6 0.7 fusion.89
  12.9 0.2 dynamic-update-slice
  13.1 15.3 %all-reduce = bf16[160]{0:T(256)(128)(2,1)S(1)} all-reduce(bf16[160]{0:T(256)(128)(2,1)S(1)} %dynamic-update-slice), channel_id=1, replica_groups=mesh['dp'=4,'ctx'=8] {'ctx'}, use_global_device_ids=true, to_apply=%add | all-reduce | flops 160 | bytes 640
  28.4 0.7 fusion.54
  29.2 14.3 %all-gather.5.cloned.1.call-done = bf16[8,20,6144]{2,1,0:T(8,128)(2,1)} async-done(((bf16[1,20,6144]{2,1,0:T(8,128)(2,1)}), bf16[8,20,6144]{2,1,0:T(8,128)(2,1)}) %all-gather.5.cloned.1.call-update) | async-done | bytes 1966096 | tf_op jit(solution)/shard_map/all_gather | solution.py:48
  43.4 2.6 reshape.127
  46.0 0.0 slice-start
  46.0 4.8 fusion.16
  50.8 4.8 fusion.103
  55.7 1.9 fusion.102
  57.6 1.8 reshape.116
  59.4 1.9 multiply_reduce_fusion.5
  61.3 1.0 copy.67
  62.2 1.8 reshape.117
  64.0 1.9 multiply_reduce_fusion.4
  65.9 1.0 copy.69
  66.9 2.4 fusion.28
  69.2 1.5 fusion.14
  70.8 0.6 copy-done.7
  71.4 5.4 convolution_convert_fusion.4
  76.8 30.2 %fusion = bf16[24,6144]{1,0:T(8,128)(2,1)} fusion(bf16[160,6144]{1,0:T(8,128)(2,1)} %convolution_convert_fusion.4), kind=kCustom, calls=%all-reduce-scatter | all-reduce-scatter fusion | flops 1179649 | bytes 2261504
  106.9 2.0 collective-permute-start
  108.9 1.5 slice
  110.5 3.2 collective-permute-start.1
  113.7 2.3 fusion.21
  116.6 9.6 %concatenate = bf16[52,6144]{1,0:T(8,128)(2,1)} concatenate(bf16[4,6144]{1,0:T(4,128)(2,1)} %collective-permute-done.1, bf16[24,6144]{1,0:T(8,128)(2,1)} %collective-permute-done, bf16[24,6144]{1,0:T(8,128)(2,1)} %fusion), dimensions={0} | concatenate | bytes 1277952
  126.2 2.8 fusion.26
  129.0 0.0 all-gather.7.cloned.1.call-update
  129.1 0.0 reduce-scatter.13.cloned.1.call-start
  129.1 30.2 %all-gather.7.cloned.1.call-done = bf16[8,20,6144]{2,1,0:T(8,128)(2,1)} async-done(((bf16[1,20,6144]{2,1,0:T(8,128)(2,1)}), bf16[8,20,6144]{2,1,0:T(8,128)(2,1)}) %all-gather.7.cloned.1.call-update) | async-done | bytes 1966096 | tf_op jit(solution)/shard_map/all_gather | solution.py:49
  159.3 4.0 reshape.129
  163.3 6.0 convolution_convert_fusion
  169.3 0.0 reduce-scatter.13.cloned.1.call-update
  169.4 0.2 reduce-scatter.7.cloned.1.call-start
  169.6 5.8 fusion.17
  175.4 0.7 copy-done.10
  176.1 1.1 fusion.48
  177.2 2.6 multiply_reduce_fusion.3
  179.8 5.7 convolution_convert_fusion.3
  185.5 0.0 reduce-scatter.7.cloned.1.call-update
  185.5 0.0 reduce-scatter.9.cloned.1.call-start
  185.6 2.4 multiply_reduce_fusion.2
  188.0 5.6 convolution_convert_fusion.2
  193.5 0.0 reduce-scatter.9.cloned.1.call-update
  193.6 0.0 reduce-scatter.11.cloned.1.call-start
  193.6 0.8 copy-done.11
  194.5 0.2 fusion.15
  194.7 4.4 convolution_convert_fusion.1
  199.1 0.0 reduce-scatter.11.cloned.1.call-update
  199.2 1.0 copy-done.3
  200.2 0.4 fusion.77
  200.6 47.0 %psum.7 = f32[6144]{0:T(1024)} all-reduce(f32[6144]{0:T(1024)S(1)} %bitcast.169), channel_id=1, replica_groups=mesh['dp'=4,'ctx'=8] {'dp','ctx'}, use_global_device_ids=true, to_apply=%region_13.14 | all-reduce | flops 6144 | bytes 49152 | tf_op jit(solution)/shard_map/psum | solution.py:83
  247.6 4.4 fusion.3
  252.0 29.3 %reduce-scatter.13.cloned.1.call-done = bf16[512,1536]{1,0:T(8,128)(2,1)} async-done(((bf16[512,6144]{1,0:T(8,128)(2,1)}), bf16[512,1536]{1,0:T(8,128)(2,1)}) %reduce-scatter.13.cloned.1.call-update) | async-done | bytes 1572880 | tf_op jit(solution)/shard_map/reduce_scatter | solution.py:125
  281.3 114.0 %reduce-scatter.7.cloned.1.call-done = bf16[1536,512]{1,0:T(8,128)(2,1)} async-done(((bf16[6144,512]{1,0:T(8,128)(2,1)}), bf16[1536,512]{1,0:T(8,128)(2,1)}) %reduce-scatter.7.cloned.1.call-update) | async-done | bytes 1572880 | tf_op jit(solution)/shard_map/reduce_scatter | solution.py:116
  395.3 114.0 %reduce-scatter.9.cloned.1.call-done = bf16[1536,512]{1,0:T(8,128)(2,1)} async-done(((bf16[6144,512]{1,0:T(8,128)(2,1)}), bf16[1536,512]{1,0:T(8,128)(2,1)}) %reduce-scatter.9.cloned.1.call-update) | async-done | bytes 1572880 | tf_op jit(solution)/shard_map/reduce_scatter | solution.py:119
  509.3 114.0 %reduce-scatter.11.cloned.1.call-done = bf16[1536,512]{1,0:T(8,128)(2,1)} async-done(((bf16[6144,512]{1,0:T(8,128)(2,1)}), bf16[1536,512]{1,0:T(8,128)(2,1)}) %reduce-scatter.11.cloned.1.call-update) | async-done | bytes 1572880 | tf_op jit(solution)/shard_map/reduce_scatter | solution.py:122
  (45 shorter events, 0.1 us)
Async XLA Ops:
  7.2 119.0 %copy-start = (bf16[1,128,6144]{2,1,0:T(8,128)(2,1)S(1)}, bf16[1,128,6144]{2,1,0:T(8,128)(2,1)}, u32[]{:S(2)}) copy-start(bf16[1,128,6144]{2,1,0:T(8,128)(2,1)} %param.10) | copy-start | bytes 4718596
  7.2 4.4 copy-start.18
  7.2 36.2 %all-gather.5.cloned.1.call-start = ((), (), s32[]{:S(2)}) async-start(), calls=%async_computation.8 | async-start | bytes 2654208 | tf_op jit(solution)/shard_map/all_gather | solution.py:48
  8.7 20.5 %copy-start.12 = (pred[20]{0:T(512)(128)(4,1)}, pred[20]{0:T(512)(128)(4,1)S(1)}, u32[]{:S(2)}) copy-start(pred[20]{0:T(512)(128)(4,1)S(1)} %get-tuple-element.7) | copy-start | bytes 64
  8.7 20.5 %copy-start.14 = (s32[20]{0:T(128)}, s32[20]{0:T(128)S(1)}, u32[]{:S(2)}) copy-start(s32[20]{0:T(128)S(1)} %get-tuple-element.8) | copy-start | bytes 244
  10.6 18.6 %copy-start.2 = (f32[20,6144]{1,0:T(8,128)}, f32[20,6144]{1,0:T(8,128)S(1)}, u32[]{:S(2)}) copy-start(f32[20,6144]{1,0:T(8,128)S(1)} %get-tuple-element.14) | copy-start | bytes 1474564
  11.5 147.8 %all-gather.7.cloned.1.call-start = ((), (), s32[]{:S(2)}) async-start(), calls=%async_computation.9 | async-start | bytes 2654208 | tf_op jit(solution)/shard_map/all_gather | solution.py:49
  46.0 9.6 %slice-start = ((s8[6291456]{0:T(1024)(128)(4,1)}), s8[4194304]{0:T(1024)(128)(4,1)S(1)}, s32[]{:S(2)}) async-start(s8[6291456]{0:T(1024)(128)(4,1)} %bitcast.167), calls=%async_computation.10 | async-start | bytes 8388608
  50.8 4.8 slice-start.1
  70.7 0.7 copy-start.7
  76.8 49.5 %copy-start.13 = (pred[20]{0:T(512)(128)(4,1)S(1)}, pred[20]{0:T(512)(128)(4,1)}, u32[]{:S(2)}) copy-start(pred[20]{0:T(512)(128)(4,1)} %copy-done.12) | copy-start | bytes 64
  76.8 49.5 %copy-start.15 = (s32[20]{0:T(128)S(1)}, s32[20]{0:T(128)}, u32[]{:S(2)}) copy-start(s32[20]{0:T(128)} %copy-done.14) | copy-start | bytes 244
  106.9 9.7 %collective-permute-start = (bf16[24,6144]{1,0:T(8,128)(2,1)}, bf16[24,6144]{1,0:T(8,128)(2,1)}, u32[]{:S(2)}, u32[]{:S(2)}) collective-permute-start(bf16[24,6144]{1,0:T(8,128)(2,1)} %fusion), channel_id=1, source_target_pairs={{0,1},{1,2},{2,3},{3,4},{4,5},{5,6},{6,7},{8,9},{9,10},{10,11},{11... | collective-permute-start | bytes 884744
  110.5 6.2 collective-permute-start.1
  129.0 34.3 %copy-start.8 = (bf16[4,20,8,128]{3,2,1,0:T(8,128)(2,1)S(1)}, bf16[4,20,8,128]{3,2,1,0:T(8,128)(2,1)}, u32[]{:S(2)}) copy-start(bf16[4,20,8,128]{3,2,1,0:T(8,128)(2,1)} %copy-done.7) | copy-start | bytes 491524
  129.1 152.3 %reduce-scatter.13.cloned.1.call-start = ((), (), s32[]{:S(2)}) async-start(), calls=%async_computation.7 | async-start | bytes 7864320 | tf_op jit(solution)/shard_map/reduce_scatter | solution.py:125
  169.4 6.8 %copy-start.9 = (bf16[20,4,8,128]{3,2,1,0:T(8,128)(2,1)S(1)}, bf16[20,4,8,128]{3,2,1,0:T(8,128)(2,1)}, u32[]{:S(2)}) copy-start(bf16[20,4,8,128]{3,2,1,0:T(8,128)(2,1)} %fusion.16) | copy-start | bytes 491524
  169.4 7.8 %copy-start.4 = (f32[160,512]{1,0:T(8,128)S(1)}, f32[160,512]{1,0:T(8,128)}, u32[]{:S(2)}) copy-start(f32[160,512]{1,0:T(8,128)} %fusion.103) | copy-start | bytes 983044
  169.4 7.8 %copy-start.5 = (f32[160,512]{1,0:T(8,128)S(1)}, f32[160,512]{1,0:T(8,128)}, u32[]{:S(2)}) copy-start(f32[160,512]{1,0:T(8,128)} %fusion.102) | copy-start | bytes 983044
  169.4 7.8 %copy-start.6 = (f32[4,160,160]{1,2,0:T(8,128)S(1)}, f32[4,160,160]{1,2,0:T(8,128)}, u32[]{:S(2)}) copy-start(f32[4,160,160]{1,2,0:T(8,128)} %fusion.28) | copy-start | bytes 1228804
  169.4 225.9 %reduce-scatter.7.cloned.1.call-start = ((), (), s32[]{:S(2)}) async-start(), calls=%async_computation.4 | async-start | bytes 7864320 | tf_op jit(solution)/shard_map/reduce_scatter | solution.py:116
  175.4 0.7 copy-start.10
  185.5 323.8 %reduce-scatter.9.cloned.1.call-start = ((), (), s32[]{:S(2)}) async-start(), calls=%async_computation.5 | async-start | bytes 7864320 | tf_op jit(solution)/shard_map/reduce_scatter | solution.py:119
  193.5 0.9 copy-start.11
  193.6 429.8 %reduce-scatter.11.cloned.1.call-start = ((), (), s32[]{:S(2)}) async-start(), calls=%async_computation.6 | async-start | bytes 7864320 | tf_op jit(solution)/shard_map/reduce_scatter | solution.py:122
  199.1 1.1 copy-start.3
  199.1 1.1 copy-start.16
  199.1 1.1 copy-start.17
  199.2 424.2 %copy-start.1 = (bf16[1,128,6144]{2,1,0:T(8,128)(2,1)S(1)}, bf16[1,128,6144]{2,1,0:T(8,128)(2,1)}, u32[]{:S(2)}) copy-start(bf16[1,128,6144]{2,1,0:T(8,128)(2,1)} %param.10) | copy-start | bytes 4718596
Sparse Core Ops, SparseCore 0:
  11.6 31.7 all-gather.4
  129.2 30.0 all-gather.6
  169.5 111.7 reduce-scatter.12
  284.1 111.2 reduce-scatter.6
  398.0 111.2 reduce-scatter.8
  512.1 111.2 reduce-scatter.10
where the time goes:
time: 632 us; the launch traced here: 630 us
  waiting for transfers between devices  416 us (66%)
  blocking collectives  92.5 us (15%)
  matrix products  66.3 us (10%)
  local copies, waits for them, and re-layouts  27.4 us (4%)
  between operations  16.4 us (3%)
    reduce_scatter x1, waiting for transfers between devices, body(): lax.psum_scatter(value_term.astype(jnp.bfloat16), 'dp', scatter_dimension...  114 us
    reduce_scatter x1, waiting for transfers between devices, body(): lax.psum_scatter(key_term.astype(jnp.bfloat16), 'dp', scatter_dimension=0...  114 us
    reduce_scatter x1, waiting for transfers between devices, body(): lax.psum_scatter(query_term.astype(jnp.bfloat16), 'dp', scatter_dimension...  114 us
    psum x1, blocking collectives, body(): grad_router = lax.psum(router_part, ('dp', 'ctx'))  47 us
    unnamed x2, blocking collectives  45.5 us
    all_gather x1, waiting for transfers between devices, body(): lax.all_gather(delta, 'ctx', axis=0, tiled=True)  30.2 us
    reduce_scatter x1, waiting for transfers between devices, body(): lax.psum_scatter(out_term.astype(jnp.bfloat16), 'dp', scatter_dimension=1...  29.3 us
    unnamed x49, local copies, waits for them, and re-layouts  21.9 us
  transfers between devices with their start and end apart: 8, of which 6 were waited for; matrix products, arithmetic and copies ran while one was open for 6% of the time, Pallas kernels for 0%

commit v1 on v0

--- a/solution.py
+++ b/solution.py
@@ -80,7 +80,7 @@
     layer_out = (tokens[0].astype(jnp.float32) + spread).astype(jnp.bfloat16)[None]
     gate_back = jnp.sum(rows_back * update, axis=-1) * weights * (1.0 - weights)
     router_part = jnp.dot(gate_back, rows, precision=HIGHEST_PRECISION)
-    grad_router = lax.psum(router_part, ("dp", "ctx"))
+    grad_router = lax.psum(lax.psum(router_part, "ctx"), "dp")
     out_term = rounded_term(
         lax.dot_general(mixed, all_delta, ROW_CONTRACT, preferred_element_type=jnp.float32)
     )

time: 632 us -> 632 us (level)
    psum x1 -> x2, blocking collectives: 47 us -> 46.6 us  [body(): grad_router = lax.psum(lax.psum(router_part, 'ctx'), 'dp')]
where the time goes in v1:
time: 632 us; the launch traced here: 630 us
  waiting for transfers between devices  417 us (66%)
  blocking collectives  92.1 us (15%)
  matrix products  66.3 us (10%)
  local copies, waits for them, and re-layouts  27.2 us (4%)
  between operations  16.4 us (3%)
    reduce_scatter x1, waiting for transfers between devices, body(): lax.psum_scatter(query_term.astype(jnp.bfloat16), 'dp', scatter_dimension...  114 us
    reduce_scatter x1, waiting for transfers between devices, body(): lax.psum_scatter(value_term.astype(jnp.bfloat16), 'dp', scatter_dimension...  114 us
    reduce_scatter x1, waiting for transfers between devices, body(): lax.psum_scatter(key_term.astype(jnp.bfloat16), 'dp', scatter_dimension=0...  114 us
    psum x2, blocking collectives, body(): grad_router = lax.psum(lax.psum(router_part, 'ctx'), 'dp')  46.6 us
    unnamed x2, blocking collectives  45.5 us
    all_gather x1, waiting for transfers between devices, body(): lax.all_gather(delta, 'ctx', axis=0, tiled=True)  30.3 us
    reduce_scatter x1, waiting for transfers between devices, body(): lax.psum_scatter(out_term.astype(jnp.bfloat16), 'dp', scatter_dimension=1...  29.7 us
    unnamed x49, local copies, waits for them, and re-layouts  21.7 us
  transfers between devices with their start and end apart: 8, of which 6 were waited for; matrix products, arithmetic and copies ran while one was open for 6% of the time, Pallas kernels for 0%

profile of v1, /device:TPU:0, one launch (start us, length us, event | category | flops | bytes accessed | tf_op | source)
XLA Modules:
  0.0 630.2 jit_solution(6419018808775178363)
XLA Ops:
  7.2 0.0 copy-start
  7.2 0.0 all-gather.5.cloned.1.call-start
  8.0 0.7 fusion.88
  8.7 1.9 multiply_reduce_fusion.1
  10.6 0.9 fusion.31
  11.5 0.0 all-gather.5.cloned.1.call-update
  11.5 0.0 all-gather.7.cloned.1.call-start
  11.6 0.6 fusion.89
  12.9 0.2 dynamic-update-slice
  13.1 15.3 %all-reduce = bf16[160]{0:T(256)(128)(2,1)S(1)} all-reduce(bf16[160]{0:T(256)(128)(2,1)S(1)} %dynamic-update-slice), channel_id=1, replica_groups=mesh['dp'=4,'ctx'=8] {'ctx'}, use_global_device_ids=true, to_apply=%add | all-reduce | flops 160 | bytes 640
  28.4 0.7 fusion.54
  29.1 14.3 %all-gather.5.cloned.1.call-done = bf16[8,20,6144]{2,1,0:T(8,128)(2,1)} async-done(((bf16[1,20,6144]{2,1,0:T(8,128)(2,1)}), bf16[8,20,6144]{2,1,0:T(8,128)(2,1)}) %all-gather.5.cloned.1.call-update) | async-done | bytes 1966096 | tf_op jit(solution)/shard_map/all_gather | solution.py:48
  43.4 2.6 reshape.127
  46.0 4.8 fusion.16
  50.8 4.8 fusion.103
  55.7 2.0 fusion.102
  57.6 1.8 reshape.116
  59.4 1.9 multiply_reduce_fusion.5
  61.3 1.0 copy.67
  62.3 1.8 reshape.117
  64.1 1.9 multiply_reduce_fusion.4
  65.9 1.0 copy.69
  66.9 2.4 fusion.28
  69.3 1.5 fusion.14
  70.8 0.7 copy-done.7
  71.4 5.3 convolution_convert_fusion.4
  76.8 30.2 %fusion = bf16[24,6144]{1,0:T(8,128)(2,1)} fusion(bf16[160,6144]{1,0:T(8,128)(2,1)} %convolution_convert_fusion.4), kind=kCustom, calls=%all-reduce-scatter | all-reduce-scatter fusion | flops 1179649 | bytes 2261504
  107.0 2.0 collective-permute-start
  108.9 1.5 slice
  110.5 3.2 collective-permute-start.1
  113.7 2.3 fusion.21
  116.6 9.5 %concatenate = bf16[52,6144]{1,0:T(8,128)(2,1)} concatenate(bf16[4,6144]{1,0:T(4,128)(2,1)} %collective-permute-done.1, bf16[24,6144]{1,0:T(8,128)(2,1)} %collective-permute-done, bf16[24,6144]{1,0:T(8,128)(2,1)} %fusion), dimensions={0} | concatenate | bytes 1277952
  126.1 2.8 fusion.26
  128.9 0.0 all-gather.7.cloned.1.call-update
  128.9 0.0 reduce-scatter.13.cloned.1.call-start
  129.0 30.3 %all-gather.7.cloned.1.call-done = bf16[8,20,6144]{2,1,0:T(8,128)(2,1)} async-done(((bf16[1,20,6144]{2,1,0:T(8,128)(2,1)}), bf16[8,20,6144]{2,1,0:T(8,128)(2,1)}) %all-gather.7.cloned.1.call-update) | async-done | bytes 1966096 | tf_op jit(solution)/shard_map/all_gather | solution.py:49
  159.2 4.0 reshape.129
  163.2 6.1 convolution_convert_fusion
  169.3 0.0 reduce-scatter.13.cloned.1.call-update
  169.3 0.2 reduce-scatter.7.cloned.1.call-start
  169.6 5.8 fusion.17
  175.4 0.7 copy-done.10
  176.0 1.1 fusion.48
  177.1 2.6 multiply_reduce_fusion.3
  179.7 5.6 convolution_convert_fusion.3
  185.4 0.0 reduce-scatter.7.cloned.1.call-update
  185.4 0.0 reduce-scatter.9.cloned.1.call-start
  185.5 2.4 multiply_reduce_fusion.2
  187.8 5.6 convolution_convert_fusion.2
  193.5 0.0 reduce-scatter.9.cloned.1.call-update
  193.5 0.0 reduce-scatter.11.cloned.1.call-start
  193.5 0.8 copy-done.11
  194.4 0.2 fusion.15
  194.6 4.4 convolution_convert_fusion.1
  199.1 0.0 reduce-scatter.11.cloned.1.call-update
  199.1 1.0 copy-done.3
  200.1 0.4 fusion.77
  200.5 25.0 %psum.14 = f32[6144]{0:T(1024)S(1)} all-reduce(f32[6144]{0:T(1024)S(1)} %bitcast.169), channel_id=1, replica_groups=mesh['dp'=4,'ctx'=8] {'ctx'}, use_global_device_ids=true, to_apply=%region_13.14 | all-reduce | flops 6144 | bytes 49152 | tf_op jit(solution)/shard_map/psum | solution.py:83
  225.5 21.7 %psum.15 = f32[6144]{0:T(1024)} all-reduce(f32[6144]{0:T(1024)S(1)} %psum.14), channel_id=1, replica_groups=mesh['dp'=4,'ctx'=8] {'dp'}, use_global_device_ids=true, to_apply=%region_14.15 | all-reduce | flops 6144 | bytes 49152 | tf_op jit(solution)/shard_map/psum | solution.py:83
  247.2 4.4 fusion.3
  251.5 29.7 %reduce-scatter.13.cloned.1.call-done = bf16[512,1536]{1,0:T(8,128)(2,1)} async-done(((bf16[512,6144]{1,0:T(8,128)(2,1)}), bf16[512,1536]{1,0:T(8,128)(2,1)}) %reduce-scatter.13.cloned.1.call-update) | async-done | bytes 1572880 | tf_op jit(solution)/shard_map/reduce_scatter | solution.py:125
  281.3 114.0 %reduce-scatter.7.cloned.1.call-done = bf16[1536,512]{1,0:T(8,128)(2,1)} async-done(((bf16[6144,512]{1,0:T(8,128)(2,1)}), bf16[1536,512]{1,0:T(8,128)(2,1)}) %reduce-scatter.7.cloned.1.call-update) | async-done | bytes 1572880 | tf_op jit(solution)/shard_map/reduce_scatter | solution.py:116
  395.3 114.0 %reduce-scatter.9.cloned.1.call-done = bf16[1536,512]{1,0:T(8,128)(2,1)} async-done(((bf16[6144,512]{1,0:T(8,128)(2,1)}), bf16[1536,512]{1,0:T(8,128)(2,1)}) %reduce-scatter.9.cloned.1.call-update) | async-done | bytes 1572880 | tf_op jit(solution)/shard_map/reduce_scatter | solution.py:119
  509.3 114.0 %reduce-scatter.11.cloned.1.call-done = bf16[1536,512]{1,0:T(8,128)(2,1)} async-done(((bf16[6144,512]{1,0:T(8,128)(2,1)}), bf16[1536,512]{1,0:T(8,128)(2,1)}) %reduce-scatter.11.cloned.1.call-update) | async-done | bytes 1572880 | tf_op jit(solution)/shard_map/reduce_scatter | solution.py:122
  (46 shorter events, 0.1 us)
Async XLA Ops:
  7.2 118.9 %copy-start = (bf16[1,128,6144]{2,1,0:T(8,128)(2,1)S(1)}, bf16[1,128,6144]{2,1,0:T(8,128)(2,1)}, u32[]{:S(2)}) copy-start(bf16[1,128,6144]{2,1,0:T(8,128)(2,1)} %param.10) | copy-start | bytes 4718596
  7.2 4.4 copy-start.18
  7.2 36.2 %all-gather.5.cloned.1.call-start = ((), (), s32[]{:S(2)}) async-start(), calls=%async_computation.8 | async-start | bytes 2654208 | tf_op jit(solution)/shard_map/all_gather | solution.py:48
  8.7 20.4 %copy-start.12 = (pred[20]{0:T(512)(128)(4,1)}, pred[20]{0:T(512)(128)(4,1)S(1)}, u32[]{:S(2)}) copy-start(pred[20]{0:T(512)(128)(4,1)S(1)} %get-tuple-element.7) | copy-start | bytes 64
  8.7 20.4 %copy-start.14 = (s32[20]{0:T(128)}, s32[20]{0:T(128)S(1)}, u32[]{:S(2)}) copy-start(s32[20]{0:T(128)S(1)} %get-tuple-element.8) | copy-start | bytes 244
  10.6 18.5 %copy-start.2 = (f32[20,6144]{1,0:T(8,128)}, f32[20,6144]{1,0:T(8,128)S(1)}, u32[]{:S(2)}) copy-start(f32[20,6144]{1,0:T(8,128)S(1)} %get-tuple-element.14) | copy-start | bytes 1474564
  11.5 147.7 %all-gather.7.cloned.1.call-start = ((), (), s32[]{:S(2)}) async-start(), calls=%async_computation.9 | async-start | bytes 2654208 | tf_op jit(solution)/shard_map/all_gather | solution.py:49
  46.0 9.6 %slice-start = ((s8[6291456]{0:T(1024)(128)(4,1)}), s8[4194304]{0:T(1024)(128)(4,1)S(1)}, s32[]{:S(2)}) async-start(s8[6291456]{0:T(1024)(128)(4,1)} %bitcast.167), calls=%async_computation.10 | async-start | bytes 8388608
  50.8 4.8 slice-start.1
  70.8 0.7 copy-start.7
  76.8 49.3 %copy-start.13 = (pred[20]{0:T(512)(128)(4,1)S(1)}, pred[20]{0:T(512)(128)(4,1)}, u32[]{:S(2)}) copy-start(pred[20]{0:T(512)(128)(4,1)} %copy-done.12) | copy-start | bytes 64
  76.8 49.3 %copy-start.15 = (s32[20]{0:T(128)S(1)}, s32[20]{0:T(128)}, u32[]{:S(2)}) copy-start(s32[20]{0:T(128)} %copy-done.14) | copy-start | bytes 244
  107.0 9.6 %collective-permute-start = (bf16[24,6144]{1,0:T(8,128)(2,1)}, bf16[24,6144]{1,0:T(8,128)(2,1)}, u32[]{:S(2)}, u32[]{:S(2)}) collective-permute-start(bf16[24,6144]{1,0:T(8,128)(2,1)} %fusion), channel_id=1, source_target_pairs={{0,1},{1,2},{2,3},{3,4},{4,5},{5,6},{6,7},{8,9},{9,10},{10,11},{11... | collective-permute-start | bytes 884744
  110.5 6.1 collective-permute-start.1
  128.9 34.3 %copy-start.8 = (bf16[4,20,8,128]{3,2,1,0:T(8,128)(2,1)S(1)}, bf16[4,20,8,128]{3,2,1,0:T(8,128)(2,1)}, u32[]{:S(2)}) copy-start(bf16[4,20,8,128]{3,2,1,0:T(8,128)(2,1)} %copy-done.7) | copy-start | bytes 491524
  128.9 152.3 %reduce-scatter.13.cloned.1.call-start = ((), (), s32[]{:S(2)}) async-start(), calls=%async_computation.7 | async-start | bytes 7864320 | tf_op jit(solution)/shard_map/reduce_scatter | solution.py:125
  169.3 6.7 %copy-start.9 = (bf16[20,4,8,128]{3,2,1,0:T(8,128)(2,1)S(1)}, bf16[20,4,8,128]{3,2,1,0:T(8,128)(2,1)}, u32[]{:S(2)}) copy-start(bf16[20,4,8,128]{3,2,1,0:T(8,128)(2,1)} %fusion.16) | copy-start | bytes 491524
  169.3 7.8 %copy-start.4 = (f32[160,512]{1,0:T(8,128)S(1)}, f32[160,512]{1,0:T(8,128)}, u32[]{:S(2)}) copy-start(f32[160,512]{1,0:T(8,128)} %fusion.103) | copy-start | bytes 983044
  169.3 7.8 %copy-start.5 = (f32[160,512]{1,0:T(8,128)S(1)}, f32[160,512]{1,0:T(8,128)}, u32[]{:S(2)}) copy-start(f32[160,512]{1,0:T(8,128)} %fusion.102) | copy-start | bytes 983044
  169.3 7.8 %copy-start.6 = (f32[4,160,160]{1,2,0:T(8,128)S(1)}, f32[4,160,160]{1,2,0:T(8,128)}, u32[]{:S(2)}) copy-start(f32[4,160,160]{1,2,0:T(8,128)} %fusion.28) | copy-start | bytes 1228804
  169.3 226.0 %reduce-scatter.7.cloned.1.call-start = ((), (), s32[]{:S(2)}) async-start(), calls=%async_computation.4 | async-start | bytes 7864320 | tf_op jit(solution)/shard_map/reduce_scatter | solution.py:116
  175.4 0.7 copy-start.10
  185.4 323.9 %reduce-scatter.9.cloned.1.call-start = ((), (), s32[]{:S(2)}) async-start(), calls=%async_computation.5 | async-start | bytes 7864320 | tf_op jit(solution)/shard_map/reduce_scatter | solution.py:119
  193.5 0.9 copy-start.11
  193.5 429.9 %reduce-scatter.11.cloned.1.call-start = ((), (), s32[]{:S(2)}) async-start(), calls=%async_computation.6 | async-start | bytes 7864320 | tf_op jit(solution)/shard_map/reduce_scatter | solution.py:122
  199.1 1.1 copy-start.3
  199.1 1.1 copy-start.16
  199.1 1.1 copy-start.17
  199.1 424.3 %copy-start.1 = (bf16[1,128,6144]{2,1,0:T(8,128)(2,1)S(1)}, bf16[1,128,6144]{2,1,0:T(8,128)(2,1)}, u32[]{:S(2)}) copy-start(bf16[1,128,6144]{2,1,0:T(8,128)(2,1)} %param.10) | copy-start | bytes 4718596
Sparse Core Ops, SparseCore 0:
  11.6 31.7 all-gather.4
  129.0 30.1 all-gather.6
  169.4 111.7 reduce-scatter.12
  284.0 111.2 reduce-scatter.6
  398.0 111.2 reduce-scatter.8
  512.1 111.2 reduce-scatter.10
